TPU v7x, 512 devices: a whole 4x4x16 slice. The times are simulated.
512 devices in a mesh: pix: 64 (over z, x), tm: 8 (over y, core).
Axes of the slice: x: 4, y: 4, z: 16, core: 2. Of those that a mesh axis runs over, the one named last changes fastest.
Arguments:
- movie: bfloat16 [131072, 2048], P('pix', 'tm'), may hold values from -6 to 6
- traces: bfloat16 [2048, 2048], P('pix', 'tm'), may hold values from 0 to 2
- footprints: bfloat16 [16384, 128], P('pix'), may hold values from 0 to 0.2
- slot_block: int32 [16384], P('pix'), may hold values from 0 to 15
- slot_neuron: int32 [16384], P('pix'), may hold values from 0 to 31
- bucket_fill: int32 [64, 64], P('pix'), may hold values from 1 to 4, as said below
Outputs:
- traces_new: bfloat16 [2048, 2048], P('pix', 'tm')
- footprints_new: float32 [16384, 128], P('pix')
Inputs may be any that keep to these rules, and one draw needn't show every extreme that they name: `bucket_fill`: A tile has at most 4 used slots for one owner; in every draw some owner gets 4 from every tile, and every tile fills 4 for some owner.
All inputs are finite; a program needn't handle non-finite values.
Results may differ from a plain program's by a relative error of at most 0.0049.
Values may be sent and summed in bfloat16 or wider, within the bound.
No kernel may reach another device: no remote copies, remote signals or barrier semaphores. Data moves between devices by JAX's collectives and lax.ppermute only.
A program may use at most 64 MiB of HBM per device.

v0:
```python
import jax
import jax.numpy as jnp
from jax import lax
from jax.sharding import PartitionSpec as P

BLOCK = 128


def local(movie, traces, footprints, slot_block, slot_neuron, bucket_fill):
    pix_count = lax.axis_size("pix")
    slot_total = footprints.shape[0]
    capacity = slot_total // pix_count
    neur_local = traces.shape[0]
    block_count = movie.shape[0] // BLOCK
    slot_index = jnp.arange(slot_total, dtype=jnp.int32)
    bucket_of = slot_index // capacity
    position = slot_index % capacity
    owner_match = bucket_of[:, None] == jnp.arange(pix_count, dtype=jnp.int32)[None, :]
    fill_slot = jnp.sum(jnp.where(owner_match, bucket_fill[0][None, :], 0), axis=1)
    usable = position < fill_slot
    masked = footprints * usable[:, None].astype(jnp.bfloat16)
    block_pick = slot_block[:, None] == jnp.arange(block_count, dtype=jnp.int32)[None, :]
    dense_map = (block_pick.astype(jnp.bfloat16)[:, :, None] * masked[:, None, :]).reshape(
        slot_total, block_count * BLOCK
    )
    asked_ids = lax.all_to_all(
        slot_neuron.reshape(pix_count, capacity), "pix", split_axis=0, concat_axis=0, tiled=True
    )
    asked_flat = asked_ids.reshape(slot_total)

    def slot_rows(source_rows):
        gathered = lax.all_gather(source_rows, "pix", axis=0, tiled=True)
        global_row = bucket_of * neur_local + slot_neuron
        return gathered[global_row]

    def residual_of(slot_traces):
        rebuilt = lax.dot_general(
            dense_map, slot_traces, (((0,), (0,)), ((), ())), preferred_element_type=jnp.float32
        )
        return (movie.astype(jnp.float32) - rebuilt).astype(jnp.bfloat16)

    slot_traces = slot_rows(traces)
    residual = residual_of(slot_traces)
    projection = jnp.dot(dense_map, residual, preferred_element_type=jnp.float32)
    slot_power = jnp.sum(masked.astype(jnp.float32) ** 2, axis=1)
    got_proj, got_power = (
        lax.all_to_all(
            projection.reshape(pix_count, capacity, projection.shape[1]),
            "pix",
            split_axis=0,
            concat_axis=0,
            tiled=True,
        ),
        lax.all_to_all(
            slot_power.reshape(pix_count, capacity), "pix", split_axis=0, concat_axis=0, tiled=True
        ),
    )
    owner_pick = (jnp.arange(neur_local, dtype=jnp.int32)[:, None] == asked_flat[None, :]).astype(
        jnp.float32
    )
    summed = jnp.dot(
        owner_pick,
        got_proj.reshape(slot_total, projection.shape[1]),
        precision=lax.Precision.HIGHEST,
    )
    power = jnp.dot(owner_pick, got_power.reshape(slot_total), precision=lax.Precision.HIGHEST)
    updated = jnp.maximum(
        0.0, traces.astype(jnp.float32) + summed / jnp.maximum(power, 0.5)[:, None]
    ).astype(jnp.bfloat16)
    slot_updated = slot_rows(updated)
    residual_two = residual_of(slot_updated)
    products = lax.dot_general(
        residual_two, slot_updated, (((1,), (1,)), ((), ())), preferred_element_type=jnp.float32
    )
    numerator = jnp.einsum(
        "bps,sb->sp",
        products.reshape(block_count, BLOCK, slot_total),
        block_pick.astype(jnp.float32),
        precision=lax.Precision.HIGHEST,
    )
    trace_power = jnp.sum(slot_updated.astype(jnp.float32) ** 2, axis=1)
    numer_all, power_all = lax.psum((numerator, trace_power), "tm")
    grown = jnp.maximum(0.0, masked.astype(jnp.float32) + numer_all / (power_all + 1e-06)[:, None])
    return (updated, jnp.where(usable[:, None], grown, 0.0))


def solution(mesh):
    return jax.shard_map(
        local,
        mesh=mesh,
        in_specs=(
            P("pix", "tm"),
            P("pix", "tm"),
            P("pix", None),
            P("pix"),
            P("pix"),
            P("pix", None),
        ),
        out_specs=(P("pix", "tm"), P("pix", None)),
        check_vma=False,
    )
```

profile of v0, /device:TPU:2, one launch (start us, length us, event | category | flops | bytes accessed | tf_op | source)
XLA Modules:
  0.0 437.4 jit_solution(8261402427538340543)
XLA Ops:
  7.9 1.4 all_to_all.15
  9.3 18.6 %all-to-all-start = ((s32[64,1,4]{2,1,0:T(1,128)}), s32[64,1,4]{2,1,0:T(1,128)S(1)}, u32[]{:S(2)}, u32[]{:S(2)}) async-start(s32[64,1,4]{2,1,0:T(1,128)} %bitcast), calls=%async_computation | async-start | bytes 65536 | tf_op jit(solution)/shard_map/all_to_all | solution.py:26
  27.9 0.7 select_reduce_fusion
  29.4 0.8 fusion.24
  30.2 1.0 fusion.21
  32.9 121.4 %all-gather.3.cloned.1.call-done = bf16[2048,256]{1,0:T(8,128)(2,1)} async-done(((bf16[32,256]{1,0:T(8,128)(2,1)}), bf16[2048,256]{1,0:T(8,128)(2,1)}) %all-gather.3.cloned.1.call-update) | async-done | bytes 1048592 | tf_op jit(solution)/shard_map/all_gather | solution.py:32
  154.3 2.3 gather_fusion
  156.7 11.4 %all-to-all-start.2 = ((f32[64,1,4]{2,1,0:T(1,128)}), f32[64,1,4]{2,1,0:T(1,128)S(1)}, u32[]{:S(2)}, u32[]{:S(2)}) async-start(f32[64,1,4]{2,1,0:T(1,128)} %bitcast.3), calls=%async_computation.2 | async-start | bytes 65536 | tf_op jit(solution)/shard_map/all_to_all | solution.py:54
  168.1 2.0 fusion.11
  170.1 1.8 copy.16
  171.9 10.0 %all-to-all-done.2 = f32[64,1,4]{2,1,0:T(1,128)S(1)} async-done(((f32[64,1,4]{2,1,0:T(1,128)}), f32[64,1,4]{2,1,0:T(1,128)S(1)}, u32[]{:S(2)}, u32[]{:S(2)}) %all-to-all-start.2) | async-done | bytes 1056 | tf_op jit(solution)/shard_map/all_to_all | solution.py:54
  182.0 5.2 %all-to-all-start.1 = ((f32[64,4,256]{2,1,0:T(4,128)}), f32[64,4,256]{2,1,0:T(4,128)S(1)}, u32[]{:S(2)}, u32[]{:S(2)}) async-start(f32[64,4,256]{2,1,0:T(4,128)} %copy.16), calls=%async_computation.1 | async-start | bytes 524288 | tf_op jit(solution)/shard_map/all_to_all | solution.py:47
  187.8 0.7 reduce.7
  189.1 0.7 reduce.6
  190.1 15.0 %all-to-all-done.1 = f32[64,4,256]{2,1,0:T(4,128)S(1)} async-done(((f32[64,4,256]{2,1,0:T(4,128)}), f32[64,4,256]{2,1,0:T(4,128)S(1)}, u32[]{:S(2)}, u32[]{:S(2)}) %all-to-all-start.1) | async-done | bytes 262176 | tf_op jit(solution)/shard_map/all_to_all | solution.py:47
  205.2 0.8 fusion.6
  206.1 130.1 %all-gather.5.cloned.1.call-done = bf16[2048,256]{1,0:T(8,128)(2,1)} async-done(((bf16[32,256]{1,0:T(8,128)(2,1)}), bf16[2048,256]{1,0:T(8,128)(2,1)}) %all-gather.5.cloned.1.call-update) | async-done | bytes 1048592 | tf_op jit(solution)/shard_map/all_gather | solution.py:32
  336.2 2.3 gather_fusion.1
  338.7 2.1 fusion.3
  340.8 12.4 %psum.15 = f32[256]{0:T(256)S(1)} all-reduce(f32[256]{0:T(256)S(1)} %multiply_reduce_fusion), channel_id=1, replica_groups=mesh['pix'=64,'tm'=8] {'tm'}, use_global_device_ids=true, to_apply=%region_4.5 | all-reduce | flops 256 | bytes 2048 | tf_op jit(solution)/shard_map/psum | solution.py:82
  353.2 2.0 copy.18
  355.2 3.5 fusion.19
  358.7 70.4 %all-reduce.2.cloned.1.call-done = f32[256,128]{1,0:T(8,128)} async-done(((f32[256,128]{1,0:T(8,128)}), f32[256,128]{1,0:T(8,128)}) %all-reduce.2.cloned.1.call-update) | async-done | bytes 131088 | tf_op jit(solution)/shard_map/psum | solution.py:82
  429.2 1.7 fusion.23
  (26 shorter events, 4.8 us)
Async XLA Ops:
  7.2 147.2 %all-gather.3.cloned.1.call-start = ((), (), s32[]{:S(2)}) async-start(), calls=%async_computation.3 | async-start | bytes 1064960 | tf_op jit(solution)/shard_map/all_gather | solution.py:32
  9.3 147.4 %all-to-all-start = ((s32[64,1,4]{2,1,0:T(1,128)}), s32[64,1,4]{2,1,0:T(1,128)S(1)}, u32[]{:S(2)}, u32[]{:S(2)}) async-start(s32[64,1,4]{2,1,0:T(1,128)} %bitcast), calls=%async_computation | async-start | bytes 65536 | tf_op jit(solution)/shard_map/all_to_all | solution.py:26
  31.2 136.9 %copy-start = (bf16[2048,256]{1,0:T(8,128)(2,1)S(1)}, bf16[2048,256]{1,0:T(8,128)(2,1)}, u32[]{:S(2)}) copy-start(bf16[2048,256]{1,0:T(8,128)(2,1)} %param.6) | copy-start | bytes 3145732
  156.7 25.3 %all-to-all-start.2 = ((f32[64,1,4]{2,1,0:T(1,128)}), f32[64,1,4]{2,1,0:T(1,128)S(1)}, u32[]{:S(2)}, u32[]{:S(2)}) async-start(f32[64,1,4]{2,1,0:T(1,128)} %bitcast.3), calls=%async_computation.2 | async-start | bytes 65536 | tf_op jit(solution)/shard_map/all_to_all | solution.py:54
  168.1 37.1 %copy-start.1 = (bf16[32,256]{1,0:T(8,128)(2,1)S(1)}, bf16[32,256]{1,0:T(8,128)(2,1)}, u32[]{:S(2)}) copy-start(bf16[32,256]{1,0:T(8,128)(2,1)} %param.7) | copy-start | bytes 49156
  182.0 23.1 %all-to-all-start.1 = ((f32[64,4,256]{2,1,0:T(4,128)}), f32[64,4,256]{2,1,0:T(4,128)S(1)}, u32[]{:S(2)}, u32[]{:S(2)}) async-start(f32[64,4,256]{2,1,0:T(4,128)} %copy.16), calls=%async_computation.1 | async-start | bytes 524288 | tf_op jit(solution)/shard_map/all_to_all | solution.py:47
  187.2 149.0 %all-gather.5.cloned.1.call-start = ((), (), s32[]{:S(2)}) async-start(), calls=%async_computation.4 | async-start | bytes 1064960 | tf_op jit(solution)/shard_map/all_gather | solution.py:32
  206.1 223.1 %all-reduce.2.cloned.1.call-start = ((), (), s32[]{:S(2)}) async-start(), calls=%async_computation.5 | async-start | bytes 262144 | tf_op jit(solution)/shard_map/psum | solution.py:82
Sparse Core Ops, SparseCore 0:
  10.9 143.3 all-gather.2
  206.2 130.0 all-gather.4
  358.8 70.2 all-reduce.1
where the time goes:
time: 438 us; the launch traced here: 437 us
  waiting for transfers between devices  348 us (79%)
  starting transfers between devices  35.4 us (8%)
  between operations  13.9 us (3%)
  blocking collectives  12.4 us (3%)
  local copies, waits for them, and re-layouts  12.2 us (3%)
  matrix products  8.5 us (2%)
  other arithmetic  7.22 us (2%)
    all_gather x2, waiting for transfers between devices, slot_rows(): gathered = lax.all_gather(source_rows, 'pix', axis=0, tiled=True)  252 us
    psum x1, waiting for transfers between devices, local(): numer_all, power_all = lax.psum((numerator, trace_power), 'tm')  70.4 us
    all_to_all x1, starting transfers between devices, local(): lax.all_to_all(slot_neuron.reshape(pix_count, capacity), 'pix', split_axi...  18.6 us
    all_to_all x1, waiting for transfers between devices, local(): lax.all_to_all(projection.reshape(pix_count, capacity, projection.shape[1...  15 us
    psum x1, blocking collectives, local(): numer_all, power_all = lax.psum((numerator, trace_power), 'tm')  12.4 us
    all_to_all x1, starting transfers between devices, local(): lax.all_to_all(slot_power.reshape(pix_count, capacity), 'pix', split_axis...  11.4 us
    all_to_all x1, waiting for transfers between devices, local(): lax.all_to_all(slot_power.reshape(pix_count, capacity), 'pix', split_axis...  10 us
  transfers between devices with their start and end apart: 6, of which 5 were waited for; matrix products, arithmetic and copies ran while one was open for 3% of the time, Pallas kernels for 0%

commit v1 on v0

--- a/solution.py
+++ b/solution.py
@@ -29,7 +29,9 @@
     asked_flat = asked_ids.reshape(slot_total)
 
     def slot_rows(source_rows):
-        gathered = lax.all_gather(source_rows, "pix", axis=0, tiled=True)
+        gathered = jnp.concatenate(
+            lax.all_to_all(jnp.stack([source_rows] * lax.axis_size("pix")), "pix", 0, 0), axis=0
+        )
         global_row = bucket_of * neur_local + slot_neuron
         return gathered[global_row]
 

time: 438 us -> 300 us (0.68)
  waiting for transfers between devices: 348 us -> 155 us
  blocking collectives: 12.4 us -> 70.1 us
    all_gather x2 -> x0, waiting for transfers between devices: 252 us -> none  [slot_rows(): gathered = lax.all_gather(source_rows, 'pix', axis=0, tiled=True)]
    all_to_all x0 -> x1, blocking collectives: none -> 57.7 us  [slot_rows(): lax.all_to_all(jnp.stack([source_rows] * lax.axis_size('pix')), 'pix', 0, 0)]
    all_to_all x0 -> x1, waiting for transfers between devices: none -> 53.3 us  [slot_rows(): lax.all_to_all(jnp.stack([source_rows] * lax.axis_size('pix')), 'pix', 0, 0)]
    all_to_all x0 -> x1, starting transfers between devices: none -> 18.6 us  [slot_rows(): lax.all_to_all(jnp.stack([source_rows] * lax.axis_size('pix')), 'pix', 0, 0)]
    all_to_all x1, starting transfers between devices: 18.6 us -> 5.95 us  [local(): lax.all_to_all(slot_neuron.reshape(pix_count, capacity), 'pix', split_axi...]
    all_to_all x1, waiting for transfers between devices: 0.01 us -> 10.8 us  [local(): lax.all_to_all(slot_neuron.reshape(pix_count, capacity), 'pix', split_axi...]
    all_to_all x1, starting transfers between devices: 11.4 us -> 5.46 us  [local(): lax.all_to_all(slot_power.reshape(pix_count, capacity), 'pix', split_axis...]
    psum x1, waiting for transfers between devices: 70.4 us -> 65.1 us  [local(): numer_all, power_all = lax.psum((numerator, trace_power), 'tm')]
  transfers between devices with their start and end apart: 6 -> 5, of which waited for: 5 -> 5; matrix products, arithmetic and copies ran while one was open for 3% -> 3% of each run, Pallas kernels for 0% -> 0%
where the time goes in v1:
time: 300 us; the launch traced here: 299 us
  waiting for transfers between devices  155 us (52%)
  blocking collectives  70.1 us (23%)
  starting transfers between devices  35.7 us (12%)
  between operations  14.3 us (5%)
  local copies, waits for them, and re-layouts  11.1 us (4%)
  matrix products  8.42 us (3%)
  other arithmetic  4.37 us (1%)
    psum x1, waiting for transfers between devices, local(): numer_all, power_all = lax.psum((numerator, trace_power), 'tm')  65.1 us
    all_to_all x1, blocking collectives, slot_rows(): lax.all_to_all(jnp.stack([source_rows] * lax.axis_size('pix')), 'pix', 0, 0)  57.7 us
    all_to_all x1, waiting for transfers between devices, slot_rows(): lax.all_to_all(jnp.stack([source_rows] * lax.axis_size('pix')), 'pix', 0, 0)  53.3 us
    all_to_all x1, starting transfers between devices, slot_rows(): lax.all_to_all(jnp.stack([source_rows] * lax.axis_size('pix')), 'pix', 0, 0)  18.6 us
    all_to_all x1, waiting for transfers between devices, local(): lax.all_to_all(projection.reshape(pix_count, capacity, projection.shape[1...  15.9 us
    psum x1, blocking collectives, local(): numer_all, power_all = lax.psum((numerator, trace_power), 'tm')  12.4 us
    all_to_all x1, waiting for transfers between devices, local(): lax.all_to_all(slot_neuron.reshape(pix_count, capacity), 'pix', split_axi...  10.8 us
    all_to_all x1, waiting for transfers between devices, local(): lax.all_to_all(slot_power.reshape(pix_count, capacity), 'pix', split_axis...  10.3 us
  transfers between devices with their start and end apart: 5, of which 5 were waited for; matrix products, arithmetic and copies ran while one was open for 3% of the time, Pallas kernels for 0%

profile of v1, /device:TPU:2, one launch (start us, length us, event | category | flops | bytes accessed | tf_op | source)
XLA Modules:
  0.0 299.3 jit_solution(1654106559460615131)
XLA Ops:
  7.2 1.9 stack.4
  9.1 18.6 %all-to-all-start.1 = ((bf16[64,32,256]{2,1,0:T(8,128)(2,1)}), bf16[64,32,256]{2,1,0:T(8,128)(2,1)S(1)}, u32[]{:S(2)}, u32[]{:S(2)}) async-start(bf16[64,32,256]{2,1,0:T(8,128)(2,1)} %stack.4), calls=%async_computation.1 | async-start | bytes 2097152 | tf_op jit(solution)/shard_map/all_to_all | solution.py:33
  27.7 0.7 all_to_all.21
  29.6 53.3 %all-to-all-done.1 = bf16[64,32,256]{2,1,0:T(8,128)(2,1)S(1)} async-done(((bf16[64,32,256]{2,1,0:T(8,128)(2,1)}), bf16[64,32,256]{2,1,0:T(8,128)(2,1)S(1)}, u32[]{:S(2)}, u32[]{:S(2)}) %all-to-all-start.1) | async-done | bytes 1048608 | tf_op jit(solution)/shard_map/all_to_all | solution.py:33
  82.9 6.0 %all-to-all-start = ((s32[64,1,4]{2,1,0:T(1,128)}), s32[64,1,4]{2,1,0:T(1,128)S(1)}, u32[]{:S(2)}, u32[]{:S(2)}) async-start(s32[64,1,4]{2,1,0:T(1,128)} %bitcast), calls=%async_computation | async-start | bytes 65536 | tf_op jit(solution)/shard_map/all_to_all | solution.py:26
  89.6 1.1 mul.38
  90.7 1.1 gather_fusion
  91.8 10.8 %all-to-all-done = s32[64,1,4]{2,1,0:T(1,128)S(1)} async-done(((s32[64,1,4]{2,1,0:T(1,128)}), s32[64,1,4]{2,1,0:T(1,128)S(1)}, u32[]{:S(2)}, u32[]{:S(2)}) %all-to-all-start) | async-done | bytes 1056 | tf_op jit(solution)/shard_map/all_to_all | solution.py:26
  102.7 5.5 %all-to-all-start.3 = ((f32[64,1,4]{2,1,0:T(1,128)}), f32[64,1,4]{2,1,0:T(1,128)S(1)}, u32[]{:S(2)}, u32[]{:S(2)}) async-start(f32[64,1,4]{2,1,0:T(1,128)} %bitcast.4), calls=%async_computation.3 | async-start | bytes 65536 | tf_op jit(solution)/shard_map/all_to_all | solution.py:56
  108.2 2.5 fusion.11
  110.7 0.9 copy.16
  111.6 10.3 %all-to-all-done.3 = f32[64,1,4]{2,1,0:T(1,128)S(1)} async-done(((f32[64,1,4]{2,1,0:T(1,128)}), f32[64,1,4]{2,1,0:T(1,128)S(1)}, u32[]{:S(2)}, u32[]{:S(2)}) %all-to-all-start.3) | async-done | bytes 1056 | tf_op jit(solution)/shard_map/all_to_all | solution.py:56
  121.9 5.6 %all-to-all-start.2 = ((f32[64,4,256]{2,1,0:T(4,128)}), f32[64,4,256]{2,1,0:T(4,128)S(1)}, u32[]{:S(2)}, u32[]{:S(2)}) async-start(f32[64,4,256]{2,1,0:T(4,128)} %copy.16), calls=%async_computation.2 | async-start | bytes 524288 | tf_op jit(solution)/shard_map/all_to_all | solution.py:49
  128.0 0.7 reduce.7
  129.4 0.7 reduce.6
  130.3 15.9 %all-to-all-done.2 = f32[64,4,256]{2,1,0:T(4,128)S(1)} async-done(((f32[64,4,256]{2,1,0:T(4,128)}), f32[64,4,256]{2,1,0:T(4,128)S(1)}, u32[]{:S(2)}, u32[]{:S(2)}) %all-to-all-start.2) | async-done | bytes 262176 | tf_op jit(solution)/shard_map/all_to_all | solution.py:49
  146.7 57.7 %all_to_all.33 = bf16[64,32,256]{2,1,0:T(8,128)(2,1)S(1)} all-to-all(bf16[64,32,256]{2,1,0:T(8,128)(2,1)S(1)} %stack.5), channel_id=1, replica_groups=mesh['pix'=64,'tm'=8] {'pix'}, dimensions={0} | all-to-all | bytes 2097152 | tf_op jit(solution)/shard_map/all_to_all | solution.py:33
  204.4 1.2 gather_fusion.1
  205.7 2.1 fusion.3
  207.7 12.4 %psum.15 = f32[256]{0:T(256)S(1)} all-reduce(f32[256]{0:T(256)S(1)} %multiply_reduce_fusion), channel_id=1, replica_groups=mesh['pix'=64,'tm'=8] {'tm'}, use_global_device_ids=true, to_apply=%region_4.5 | all-reduce | flops 256 | bytes 2048 | tf_op jit(solution)/shard_map/psum | solution.py:84
  220.2 2.0 copy.18
  222.2 3.5 %fusion.19 = f32[256,1,128]{2,1,0:T(1,128)} fusion(f32[16,128,256]{1,0,2:T(8,128)} %copy.18, pred[256,16,1]{1,0,2:T(32,128)(4,1)S(1)} %get-tuple-element.6), kind=kOutput, calls=%fused_computation.21 | convolution fusion | flops 6291456 | bytes 2232320 | tf_op jit(solution)/shard_map/bps,sb->sp/dot_general | solution.py:77
  225.7 65.1 %all-reduce.2.cloned.1.call-done = f32[256,128]{1,0:T(8,128)} async-done(((f32[256,128]{1,0:T(8,128)}), f32[256,128]{1,0:T(8,128)}) %all-reduce.2.cloned.1.call-update) | async-done | bytes 131088 | tf_op jit(solution)/shard_map/psum | solution.py:84
  290.8 1.7 fusion.23
  (35 shorter events, 3.8 us)
Async XLA Ops:
  7.2 20.6 %copy-start.4 = (s32[256]{0:T(256)S(1)}, s32[256]{0:T(256)}, u32[]{:S(2)}) copy-start(s32[256]{0:T(256)} %param.10) | copy-start | bytes 3076
  7.2 21.3 %copy-start.6 = (s32[1,64]{1,0:T(1,128)S(1)}, s32[1,64]{1,0:T(1,128)}, u32[]{:S(2)}) copy-start(s32[1,64]{1,0:T(1,128)} %param.11) | copy-start | bytes 772
  7.2 21.4 %copy-start.5 = (s32[256]{0:T(256)S(1)}, s32[256]{0:T(256)}, u32[]{:S(2)}) copy-start(s32[256]{0:T(256)} %param.9) | copy-start | bytes 3076
  7.2 21.5 %copy-start.3 = (bf16[256,128]{1,0:T(8,128)(2,1)S(1)}, bf16[256,128]{1,0:T(8,128)(2,1)}, u32[]{:S(2)}) copy-start(bf16[256,128]{1,0:T(8,128)(2,1)} %param.8) | copy-start | bytes 196612
  9.1 73.8 %all-to-all-start.1 = ((bf16[64,32,256]{2,1,0:T(8,128)(2,1)}), bf16[64,32,256]{2,1,0:T(8,128)(2,1)S(1)}, u32[]{:S(2)}, u32[]{:S(2)}) async-start(bf16[64,32,256]{2,1,0:T(8,128)(2,1)} %stack.4), calls=%async_computation.1 | async-start | bytes 2097152 | tf_op jit(solution)/shard_map/all_to_all | solution.py:33
  28.9 79.3 %copy-start = (bf16[2048,256]{1,0:T(8,128)(2,1)S(1)}, bf16[2048,256]{1,0:T(8,128)(2,1)}, u32[]{:S(2)}) copy-start(bf16[2048,256]{1,0:T(8,128)(2,1)} %param.6) | copy-start | bytes 3145732
  82.9 19.8 %all-to-all-start = ((s32[64,1,4]{2,1,0:T(1,128)}), s32[64,1,4]{2,1,0:T(1,128)S(1)}, u32[]{:S(2)}, u32[]{:S(2)}) async-start(s32[64,1,4]{2,1,0:T(1,128)} %bitcast), calls=%async_computation | async-start | bytes 65536 | tf_op jit(solution)/shard_map/all_to_all | solution.py:26
  102.7 19.2 %all-to-all-start.3 = ((f32[64,1,4]{2,1,0:T(1,128)}), f32[64,1,4]{2,1,0:T(1,128)S(1)}, u32[]{:S(2)}, u32[]{:S(2)}) async-start(f32[64,1,4]{2,1,0:T(1,128)} %bitcast.4), calls=%async_computation.3 | async-start | bytes 65536 | tf_op jit(solution)/shard_map/all_to_all | solution.py:56
  108.1 38.2 %copy-start.1 = (bf16[32,256]{1,0:T(8,128)(2,1)S(1)}, bf16[32,256]{1,0:T(8,128)(2,1)}, u32[]{:S(2)}) copy-start(bf16[32,256]{1,0:T(8,128)(2,1)} %param.7) | copy-start | bytes 49156
  121.9 24.3 %all-to-all-start.2 = ((f32[64,4,256]{2,1,0:T(4,128)}), f32[64,4,256]{2,1,0:T(4,128)S(1)}, u32[]{:S(2)}, u32[]{:S(2)}) async-start(f32[64,4,256]{2,1,0:T(4,128)} %copy.16), calls=%async_computation.2 | async-start | bytes 524288 | tf_op jit(solution)/shard_map/all_to_all | solution.py:49
  127.5 163.3 %all-reduce.2.cloned.1.call-start = ((), (), s32[]{:S(2)}) async-start(), calls=%async_computation.5 | async-start | bytes 262144 | tf_op jit(solution)/shard_map/psum | solution.py:84
  146.6 59.0 %copy-start.2 = (bf16[32,256]{1,0:T(8,128)(2,1)}, bf16[32,256]{1,0:T(8,128)(2,1)S(1)}, u32[]{:S(2)}) copy-start(bf16[32,256]{1,0:T(8,128)(2,1)S(1)} %fusion.6) | copy-start | bytes 49156
Sparse Core Ops, SparseCore 0:
  225.8 64.9 all-reduce.1
